TPU v7x, 256 devices: a whole 4x4x8 slice. The times are simulated.
256 devices in a mesh: seq: 64 (over x, z, core), tensor: 4 (over y).
Axes of the slice: x: 4, y: 4, z: 8, core: 2. Of those that a mesh axis runs over, the one named last changes fastest.
Arguments:
- hidden: bfloat16 [512, 1280], P('seq', 'tensor'), may hold values from -20 to 20
- inward_weight: bfloat16 [1280, 3, 1280], P(None, None, 'tensor'), may hold values from -0.15625 to 0.15625
- output_weight: bfloat16 [1280, 1280], P('tensor'), may hold values from -0.559017 to 0.559017
- score_gain: float32 [1280], P('tensor'), may hold values from 0.5 to 9
- eigen_rate: float32 [1280], replicated, may hold values from 0.1 to 0.6
- lengths: int32 [512], replicated, may hold values from 1 to 16384, as said below
- page_request: int32 [1536], P('seq'), may hold values from 0 to 511, as said below
- page_number: int32 [1536], P('seq'), may hold values from 0 to 128, as said below
- page_cache: bfloat16 [1536, 128, 2, 1280], P('seq', None, None, 'tensor'), may hold values from -6 to 6
Outputs:
- new_hidden: bfloat16 [512, 1280], P('seq', 'tensor')
Inputs may be any that keep to these rules, and one draw needn't show every extreme that they name: `lengths`: exactly 4 requests have more than 256 cached positions; they have more than 16256, one has exactly 16384. Every other request has at most 256, one exactly 256. `page_request`: each page of each request stands in exactly one slot: pages 0 to 1 of every short request, pages 0 to 127 of every long request. The remaining 2 * 4 slots name a long request with page number 128 and hold nothing live. `page_number`: see page_request.
All inputs are finite; a program needn't handle non-finite values.
Results may differ from a plain program's by a relative error of at most 0.012.
The roundings to bfloat16 on the way count: a program that leaves them out, or rounds other values in their place, can miss the bound.
Values may be sent and summed in bfloat16 or wider, within the bound.
No kernel may reach another device: no remote copies, remote signals or barrier semaphores. Data moves between devices by JAX's collectives and lax.ppermute only.
A program may use at most 192 MiB of HBM per device.

v0:
```python
import math
import jax
import jax.numpy as jnp
from jax import lax
from jax.sharding import PartitionSpec as P

HEAD_DIM = 64
epsilon = 1e-06
far_below = -1e30


def head_norm(values, gain):
    shaped = values.reshape(values.shape[:-1] + (-1, HEAD_DIM))
    normed = shaped / jnp.sqrt(jnp.mean(shaped * shaped, axis=-1, keepdims=True) + epsilon)
    return normed * gain.reshape(-1, HEAD_DIM)


def scale_heads(summed, factor):
    shaped = summed.reshape(summed.shape[:-1] + (factor.shape[-1], -1))
    return (shaped * factor[..., None]).reshape(summed.shape)


def local(
    hidden,
    inward_weight,
    output_weight,
    score_gain,
    eigen_rate,
    lengths,
    page_request,
    page_number,
    page_cache,
):
    rows, width_local = hidden.shape
    heads_local = width_local // HEAD_DIM
    gathered = lax.all_gather(hidden, "tensor", axis=1, tiled=True)
    projected = jnp.dot(
        gathered,
        inward_weight.reshape(inward_weight.shape[0], -1),
        preferred_element_type=jnp.float32,
    )
    query = head_norm(projected[:, :width_local], score_gain).astype(jnp.bfloat16)
    key_new = head_norm(projected[:, width_local : 2 * width_local], score_gain).astype(
        jnp.bfloat16
    )
    value_own = projected[:, 2 * width_local :].astype(jnp.bfloat16)
    own_score = jnp.sum(
        (query.astype(jnp.float32) * key_new.astype(jnp.float32)).reshape(
            rows, heads_local, HEAD_DIM
        ),
        axis=-1,
    ) / math.sqrt(HEAD_DIM)
    all_queries = lax.all_gather(query, "seq", axis=0, tiled=True)
    pages, page_len = (page_cache.shape[0], page_cache.shape[1])
    owner_query = all_queries[page_request].reshape(pages, heads_local, HEAD_DIM)
    keys_scaled = head_norm(page_cache[:, :, 0, :].astype(jnp.float32), score_gain).astype(
        jnp.bfloat16
    )
    values_paged = page_cache[:, :, 1, :].reshape(pages, page_len, heads_local, HEAD_DIM)
    scores = jnp.einsum(
        "sphd,shd->shp", keys_scaled, owner_query, preferred_element_type=jnp.float32
    ) / math.sqrt(HEAD_DIM)
    positions = page_number[:, None] * page_len + jnp.arange(page_len, dtype=jnp.int32)[None, :]
    live_mask = positions < lengths[page_request][:, None]
    page_max = jnp.max(jnp.where(live_mask[:, None, :], scores, far_below), axis=-1)
    weights = jnp.where(live_mask[:, None, :], jnp.exp(scores - page_max[..., None]), 0.0).astype(
        jnp.bfloat16
    )
    page_total = jnp.sum(weights.astype(jnp.float32), axis=-1)
    page_acc = jnp.einsum(
        "shp,sphd->shd", weights, values_paged, preferred_element_type=jnp.float32
    ).reshape(pages, width_local)
    packed = jnp.concatenate(
        [page_acc, page_total, page_max, page_request.astype(jnp.float32)[:, None]], axis=1
    )
    all_parts = lax.all_gather(packed, "seq", axis=0, tiled=True)
    acc_all = all_parts[:, :width_local]
    total_all = all_parts[:, width_local : width_local + heads_local]
    max_all = all_parts[:, width_local + heads_local : width_local + 2 * heads_local]
    owner_all = all_parts[:, width_local + 2 * heads_local]
    first_row = lax.axis_index("seq") * rows
    row_ids = (first_row + jnp.arange(rows, dtype=jnp.int32)).astype(jnp.float32)
    mine = owner_all[None, :] == row_ids[:, None]
    masked_max = jnp.max(jnp.where(mine[:, :, None], max_all[None], far_below), axis=1)
    final_max = jnp.maximum(masked_max, own_score)
    factor = jnp.where(mine[:, :, None], jnp.exp(max_all[None] - final_max[:, None, :]), 0.0)
    own_factor = jnp.exp(own_score - final_max)
    total = jnp.sum(factor * total_all[None], axis=1) + own_factor
    stored = jnp.einsum(
        "rsh,shd->rhd",
        factor,
        acc_all.reshape(-1, heads_local, HEAD_DIM),
        precision=lax.Precision.HIGHEST,
    ).reshape(rows, width_local)
    summed = stored + scale_heads(value_own.astype(jnp.float32), own_factor)
    attended = (
        (summed.reshape(rows, heads_local, HEAD_DIM) / total[..., None])
        .reshape(rows, width_local)
        .astype(jnp.bfloat16)
    )
    partial_out = jnp.dot(attended, output_weight, preferred_element_type=jnp.float32)
    attn_out = lax.psum(partial_out, "tensor")
    width = attn_out.shape[1]
    state = gathered.astype(jnp.float32)
    unit = attn_out / jnp.sqrt(
        jnp.sum(attn_out * attn_out, axis=-1, keepdims=True) / width + epsilon
    )
    mixed = state + eigen_rate * (unit - state)
    result = mixed / jnp.sqrt(jnp.sum(mixed * mixed, axis=-1, keepdims=True) / width + epsilon)
    first_col = lax.axis_index("tensor") * width_local
    return lax.dynamic_slice_in_dim(result, first_col, width_local, 1).astype(jnp.bfloat16)


def solution(mesh):
    placed = (
        P("seq", "tensor"),
        P(None, None, "tensor"),
        P("tensor", None),
        P("tensor"),
        P(),
        P(),
        P("seq"),
        P("seq"),
        P("seq", None, None, "tensor"),
    )
    return jax.shard_map(
        local, mesh=mesh, in_specs=placed, out_specs=P("seq", "tensor"), check_vma=False
    )
```

profile of v0, /device:TPU:4, one launch (start us, length us, event | category | flops | bytes accessed | tf_op | source)
XLA Modules:
  0.0 202.5 jit_solution(14112942308790230901)
XLA Ops:
  6.5 0.8 broadcast_multiply_fusion
  7.3 0.7 compare_select_fusion
  8.1 0.8 mul.86
  8.8 12.7 %all-gather = bf16[4,320,8]{1,2,0:T(8,128)(2,1)S(1)} all-gather(bf16[1,320,8]{1,2,0:T(8,128)(2,1)} %bitcast.52), channel_id=1, replica_groups=mesh['seq'=64,'tensor'=4] {'tensor'}, dimensions={0}, use_global_device_ids=true | all-gather | bytes 25600 | tf_op jit(solution)/shard_map/all_gather | solution.py:36
  21.5 0.1 reshape.184
  21.7 0.7 fusion.21
  22.5 0.6 copy-done.3
  23.1 0.1 multiply_reduce_fusion.5
  23.3 0.1 multiply_reduce_fusion.4
  23.4 0.2 multiply_reduce_fusion.3
  23.6 53.2 %all_gather.10 = bf16[512,5,64]{2,0,1:T(8,128)(2,1)S(1)} all-gather(bf16[8,5,64]{2,0,1:T(8,128)(2,1)S(1)} %copy.50), channel_id=1, replica_groups=mesh['seq'=64,'tensor'=4] {'seq'}, dimensions={0}, use_global_device_ids=true | all-gather | bytes 332800 | tf_op jit(solution)/shard_map/all_gather | solution.py:53
  76.8 0.5 copy.51
  77.2 0.7 gather_fusion
  78.0 1.2 gather_fusion.1
  79.2 3.7 %fusion.18 = (bf16[24,128,1,320]{1,3,2,0:T(8,128)(2,1)}, bf16[24,128,1,320]{1,3,2,0:T(8,128)(2,1)S(1)}) fusion(bf16[24,128,2,320]{1,3,2,0:T(8,128)(2,1)} %param.17), kind=kLoop, calls=%fused_computation.58 | loop fusion | bytes 7864320 | tf_op jit(solution)/shard_map/slice | solution.py:59
  82.8 0.7 fusion
  83.6 0.1 add_compare_fusion
  83.7 0.7 fusion.3
  84.4 0.1 select_reduce_fusion.1
  84.5 0.2 fusion.16
  84.7 0.1 copy.53
  84.8 0.1 copy.54
  84.9 0.1 copy.52
  85.0 2.6 %fusion.9 = f32[24,5,1,64]{3,2,1,0:T(1,128)S(1)} fusion(bf16[24,128,5,64]{1,3,2,0:T(8,128)(2,1)} %bitcast.49, bf16[24,5,128,1]{2,0,1,3:T(8,128)(2,1)S(1)} %get-tuple-element.15), kind=kOutput, calls=%fused_computation.20 | convolution fusion | flops 1966080 | bytes 2027520 | tf_op jit(solution)/shard_map/shp,sphd->shd/dot_general | solution.py:70
  87.6 0.1 reshape.160
  87.7 0.7 pad_maximum_fusion
  88.4 0.1 copy.57
  88.5 74.1 %all-gather.3.cloned.1.call-done = f32[1536,331]{1,0:T(8,128)} async-done(((f32[24,331]{1,0:T(8,128)}), f32[1536,331]{1,0:T(8,128)}) %all-gather.3.cloned.1.call-update) | async-done | bytes 2033680 | tf_op jit(solution)/shard_map/all_gather | solution.py:76
  162.7 3.0 %fusion.19 = (f32[1536,5]{1,0:T(8,128)}, f32[1536,5]{1,0:T(8,128)S(1)}) fusion(f32[1536,331]{1,0:T(8,128)} %all-gather.3.cloned.1.call-done), kind=kLoop, calls=%fused_computation.59 | loop fusion | bytes 122880 | tf_op jit(solution)/shard_map/slice | solution.py:79
  165.6 1.4 copy.56
  167.0 0.3 copy.60
  167.3 1.6 slice_reduce_fusion
  169.0 0.1 broadcast_compare_fusion
  169.0 0.1 select_reduce_fusion
  169.1 0.2 multiply_reduce_fusion
  169.4 0.1 copy.61
  169.4 0.1 copy.59
  169.5 0.1 mul.96
  169.6 0.1 mul.97
  169.8 0.1 div.96
  169.8 3.0 %copy.55 = f32[1536,320]{0,1:T(8,128)} copy(f32[1536,320]{1,0:T(8,128)} %bitcast.45) | data formatting | bytes 3932160 | tf_op jit(solution)/shard_map/slice | solution.py:77
  172.9 3.3 %convolution_bitcast_fusion = f32[8,5,64]{2,0,1:T(8,128)S(1)} fusion(f32[1536,5,64]{0,2,1:T(8,128)} %bitcast.46, f32[8,5]{0,1:T(8,128)S(1)} %multiply_maximum_fusion, f32[1536,5]{0,1:T(8,128)S(1)} %copy.56, pred[8,1536]{1,0:T(8,128)(4,1)S(1)} %broadcast_compare_fusion), kind=kOutput, calls=%fused_computation.8 | convolution fusion | flops 47308800 | bytes 2019488 | tf_op jit(solution)/shard_map/rsh,shd->rhd/dot_general | solution.py:89
  176.2 0.1 reshape.163
  176.3 0.9 fusion.14
  177.2 17.4 %psum.7 = f32[8,1280]{1,0:T(8,128)S(1)} all-reduce(f32[8,1280]{1,0:T(8,128)S(1)} %fusion.14), channel_id=1, replica_groups=mesh['seq'=64,'tensor'=4] {'tensor'}, use_global_device_ids=true, to_apply=%region_8.9 | all-reduce | flops 10240 | bytes 81920 | tf_op jit(solution)/shard_map/psum | solution.py:102
  194.6 0.1 multiply_reduce_fusion.2
  194.7 0.2 multiply_reduce_fusion.1
  194.9 0.7 fusion.13
  (29 shorter events, 0.5 us)
Async XLA Ops:
  6.5 15.1 %copy-start = (bf16[1280,3,320]{0,2,1:T(8,128)(2,1)S(1)}, bf16[1280,3,320]{0,2,1:T(8,128)(2,1)}, u32[]{:S(2)}) copy-start(bf16[1280,3,320]{0,2,1:T(8,128)(2,1)} %param.10) | copy-start | bytes 7372804
  6.5 156.1 %all-gather.3.cloned.1.call-start = ((), (), s32[]{:S(2)}) async-start(), calls=%async_computation | async-start | bytes 2396160 | tf_op jit(solution)/shard_map/all_gather | solution.py:76
  21.6 55.6 %copy-start.1 = (s32[512]{0:T(512)S(1)}, s32[512]{0:T(512)}, u32[]{:S(2)}) copy-start(s32[512]{0:T(512)} %param.14) | copy-start | bytes 6148
  22.4 0.6 copy-start.3
  79.2 4.5 %copy-start.4 = (bf16[24,5,64]{2,1,0:T(8,128)(2,1)S(1)}, bf16[24,5,64]{2,1,0:T(8,128)(2,1)}, u32[]{:S(2)}) copy-start(bf16[24,5,64]{2,1,0:T(8,128)(2,1)} %gather_fusion.1) | copy-start | bytes 46084
  169.8 6.5 %copy-start.2 = (bf16[320,1280]{1,0:T(8,128)(2,1)S(1)}, bf16[320,1280]{1,0:T(8,128)(2,1)}, u32[]{:S(2)}) copy-start(bf16[320,1280]{1,0:T(8,128)(2,1)} %param.11) | copy-start | bytes 2457604
  172.9 21.8 %copy-start.5 = (f32[1280]{0:T(1024)S(1)}, f32[1280]{0:T(1024)}, u32[]{:S(2)}) copy-start(f32[1280]{0:T(1024)} %param.13) | copy-start | bytes 15364
Sparse Core Ops, SparseCore 0:
  88.6 74.0 all-gather.2
where the time goes:
time: 203 us; the launch traced here: 202 us
  blocking collectives  83.2 us (41%)
  waiting for transfers between devices  74.1 us (37%)
  local copies, waits for them, and re-layouts  18 us (9%)
  between operations  13.5 us (7%)
  matrix products  8.35 us (4%)
  other arithmetic  5.14 us (3%)
    all_gather x1, waiting for transfers between devices, local(): all_parts = lax.all_gather(packed, 'seq', axis=0, tiled=True)  74.1 us
    all_gather x1, blocking collectives, local(): all_queries = lax.all_gather(query, 'seq', axis=0, tiled=True)  53.2 us
    psum x1, blocking collectives, local(): attn_out = lax.psum(partial_out, 'tensor')  17.4 us
    all_gather x1, blocking collectives, local(): gathered = lax.all_gather(hidden, 'tensor', axis=1, tiled=True)  12.7 us
    slice x2, local copies, waits for them, and re-layouts, local(): all_parts[:, width_local + heads_local:width_local + 2 * heads_local]  4.38 us
  transfers between devices with their start and end apart: 1, of which 1 were waited for; matrix products, arithmetic and copies ran while one was open for 0% of the time, Pallas kernels for 0%

commit v1 on v0

--- a/solution.py
+++ b/solution.py
@@ -50,7 +50,9 @@
         ),
         axis=-1,
     ) / math.sqrt(HEAD_DIM)
-    all_queries = lax.all_gather(query, "seq", axis=0, tiled=True)
+    all_queries = jnp.concatenate(
+        lax.all_to_all(jnp.stack([query] * lax.axis_size("seq")), "seq", 0, 0), axis=0
+    )
     pages, page_len = (page_cache.shape[0], page_cache.shape[1])
     owner_query = all_queries[page_request].reshape(pages, heads_local, HEAD_DIM)
     keys_scaled = head_norm(page_cache[:, :, 0, :].astype(jnp.float32), score_gain).astype(

time: 203 us -> 170 us (0.84)
  blocking collectives: 83.2 us -> 30 us
  starting transfers between devices: 0.01 us -> 12.1 us
  waiting for transfers between devices: 74.1 us -> 77.9 us
  local copies, waits for them, and re-layouts: 18 us -> 20.5 us
    all_gather x1 -> x0, blocking collectives: 53.2 us -> none  [local(): all_queries = lax.all_gather(query, 'seq', axis=0, tiled=True)]
    all_to_all x0 -> x1, starting transfers between devices: none -> 12.1 us  [local(): lax.all_to_all(jnp.stack([query] * lax.axis_size('seq')), 'seq', 0, 0)]
    all_to_all x0 -> x1, waiting for transfers between devices: none -> 4.68 us  [local(): lax.all_to_all(jnp.stack([query] * lax.axis_size('seq')), 'seq', 0, 0)]
  transfers between devices with their start and end apart: 1 -> 2, of which waited for: 1 -> 2; matrix products, arithmetic and copies ran while one was open for 0% -> 5% of each run, Pallas kernels for 0% -> 0%
where the time goes in v1:
time: 170 us
  waiting for transfers between devices  77.9 us (46%)
  blocking collectives  30 us (18%)
  local copies, waits for them, and re-layouts  20.5 us (12%)
  between operations  13.6 us (8%)
  starting transfers between devices  12.1 us (7%)
  matrix products  9.9 us (6%)
  other arithmetic  5.77 us (3%)
    all_gather x1, waiting for transfers between devices, local(): all_parts = lax.all_gather(packed, 'seq', axis=0, tiled=True)  73.2 us
    psum x1, blocking collectives, local(): attn_out = lax.psum(partial_out, 'tensor')  17.4 us
    all_gather x1, blocking collectives, local(): gathered = lax.all_gather(hidden, 'tensor', axis=1, tiled=True)  12.7 us
    all_to_all x1, starting transfers between devices, local(): lax.all_to_all(jnp.stack([query] * lax.axis_size('seq')), 'seq', 0, 0)  12.1 us
    all_to_all x1, waiting for transfers between devices, local(): lax.all_to_all(jnp.stack([query] * lax.axis_size('seq')), 'seq', 0, 0)  4.68 us
    slice x2, local copies, waits for them, and re-layouts, local(): all_parts[:, width_local + heads_local:width_local + 2 * heads_local]  4.38 us
    slice x1, local copies, waits for them, and re-layouts, local(): page_cache[:, :, 1, :].reshape(pages, page_len, heads_local, HEAD_DIM)  4.28 us
  transfers between devices with their start and end apart: 2, of which 2 were waited for; matrix products, arithmetic and copies ran while one was open for 5% of the time, Pallas kernels for 0%

profile of v1, /device:TPU:4, one launch (start us, length us, event | category | flops | bytes accessed | tf_op | source)
XLA Modules:
  0.0 169.9 jit_solution(17696709360320352634)
XLA Ops:
  6.5 0.9 mul.88
  7.4 12.7 %all-gather = bf16[4,320,8]{1,2,0:T(8,128)(2,1)S(1)} all-gather(bf16[1,320,8]{1,2,0:T(8,128)(2,1)} %bitcast.59), channel_id=1, replica_groups=mesh['seq'=64,'tensor'=4] {'tensor'}, dimensions={0}, use_global_device_ids=true | all-gather | bytes 25600 | tf_op jit(solution)/shard_map/all_gather | solution.py:36
  20.1 0.1 reshape.191
  20.3 0.7 fusion.21
  21.1 0.6 copy-done.3
  21.7 0.1 multiply_reduce_fusion.5
  21.9 0.1 multiply_reduce_fusion.4
  22.0 0.2 multiply_reduce_fusion.3
  22.2 0.1 broadcast_bitcast_fusion
  22.3 1.1 reshape.197
  23.4 12.1 %all-to-all-start = ((bf16[64,2,1280]{2,1,0:T(2,128)(2,1)}), bf16[64,2,1280]{2,1,0:T(2,128)(2,1)S(1)}, u32[]{:S(2)}, u32[]{:S(2)}) async-start(bf16[64,2,1280]{2,1,0:T(2,128)(2,1)} %reshape.197), calls=%async_computation | async-start | bytes 655360 | tf_op jit(solution)/shard_map/all_to_all | solution.py:54
  35.6 0.1 copy.67
  35.7 4.3 %fusion.18 = (bf16[24,128,1,320]{1,3,2,0:T(8,128)(2,1)}, bf16[24,128,1,320]{1,3,2,0:T(8,128)(2,1)}) fusion(bf16[24,128,2,320]{1,3,2,0:T(8,128)(2,1)} %param.17), kind=kLoop, calls=%fused_computation.59 | loop fusion | bytes 7864320 | tf_op jit(solution)/shard_map/slice | solution.py:61
  40.0 0.7 gather_fusion
  40.7 2.2 %fusion = f32[24,128,5]{1,2,0:T(8,128)S(1)} fusion(bf16[24,128,5,64]{1,3,2,0:T(8,128)(2,1)} %bitcast.54), kind=kLoop, calls=%fused_computation.4 | loop fusion | flops 2933760 | bytes 2027520 | tf_op jit(solution)/shard_map/reduce_sum | solution.py:14
  43.0 0.7 add_sqrt_fusion
  43.7 4.7 %all-to-all-done = bf16[64,2,1280]{2,1,0:T(2,128)(2,1)S(1)} async-done(((bf16[64,2,1280]{2,1,0:T(2,128)(2,1)}), bf16[64,2,1280]{2,1,0:T(2,128)(2,1)S(1)}, u32[]{:S(2)}, u32[]{:S(2)}) %all-to-all-start) | async-done | bytes 327712 | tf_op jit(solution)/shard_map/all_to_all | solution.py:54
  48.3 0.4 reshape.198
  48.7 0.1 copy_bitcast_fusion
  48.9 0.5 copy.64
  49.4 1.2 gather_fusion.1
  50.5 2.3 %fusion.3 = f32[24,5,1,128]{3,2,1,0:T(1,128)S(1)} fusion(bf16[24,128,5,64]{1,3,2,0:T(8,128)(2,1)} %bitcast.55, f32[5,64]{1,0:T(8,128)S(1)} %mul.88, f32[24,128,5]{1,2,0:T(8,128)} %add_sqrt_fusion, bf16[24,5,64,1]{2,1,0,3:T(8,128)(2,1)} %bitcast.58), kind=kOutput, calls=%fused_computation.7 | convolution fusion | flops 5898240 | bytes 2105600 | tf_op jit(solution)/shard_map/sphd,shd->shp/dot_general | solution.py:62
  52.8 0.1 select_reduce_fusion.1
  53.0 0.2 fusion.16
  53.1 0.1 copy.66
  53.2 0.1 copy.65
  53.3 2.6 %fusion.9 = f32[24,5,1,64]{3,2,1,0:T(1,128)S(1)} fusion(bf16[24,128,5,64]{1,3,2,0:T(8,128)(2,1)} %bitcast.56, bf16[24,5,128,1]{2,0,1,3:T(8,128)(2,1)S(1)} %get-tuple-element.15), kind=kOutput, calls=%fused_computation.21 | convolution fusion | flops 1966080 | bytes 2027520 | tf_op jit(solution)/shard_map/shp,sphd->shd/dot_general | solution.py:72
  56.0 0.1 reshape.167
  56.1 0.7 pad_maximum_fusion
  56.8 0.1 copy.70
  56.9 73.2 %all-gather.3.cloned.1.call-done = f32[1536,331]{1,0:T(8,128)} async-done(((f32[24,331]{1,0:T(8,128)}), f32[1536,331]{1,0:T(8,128)}) %all-gather.3.cloned.1.call-update) | async-done | bytes 2033680 | tf_op jit(solution)/shard_map/all_gather | solution.py:78
  130.1 3.0 %fusion.19 = (f32[1536,5]{1,0:T(8,128)}, f32[1536,5]{1,0:T(8,128)S(1)}) fusion(f32[1536,331]{1,0:T(8,128)} %all-gather.3.cloned.1.call-done), kind=kLoop, calls=%fused_computation.60 | loop fusion | bytes 122880 | tf_op jit(solution)/shard_map/slice | solution.py:81
  133.1 1.4 copy.69
  134.5 0.3 copy.73
  134.7 1.6 slice_reduce_fusion
  136.4 0.1 broadcast_compare_fusion
  136.5 0.1 select_reduce_fusion
  136.6 0.2 multiply_reduce_fusion
  136.8 0.1 copy.74
  136.9 0.1 copy.72
  137.2 0.1 div.98
  137.3 3.0 %copy.68 = f32[1536,320]{0,1:T(8,128)} copy(f32[1536,320]{1,0:T(8,128)} %bitcast.52) | data formatting | bytes 3932160 | tf_op jit(solution)/shard_map/slice | solution.py:79
  140.3 3.3 %convolution_bitcast_fusion = f32[8,5,64]{2,0,1:T(8,128)S(1)} fusion(f32[1536,5,64]{0,2,1:T(8,128)} %bitcast.53, f32[8,5]{0,1:T(8,128)S(1)} %multiply_maximum_fusion, f32[1536,5]{0,1:T(8,128)S(1)} %copy.69, pred[8,1536]{1,0:T(8,128)(4,1)S(1)} %broadcast_compare_fusion), kind=kOutput, calls=%fused_computation.8 | convolution fusion | flops 47308800 | bytes 2019488 | tf_op jit(solution)/shard_map/rsh,shd->rhd/dot_general | solution.py:91
  143.7 0.9 fusion.14
  144.6 17.4 %psum.7 = f32[8,1280]{1,0:T(8,128)S(1)} all-reduce(f32[8,1280]{1,0:T(8,128)S(1)} %fusion.14), channel_id=1, replica_groups=mesh['seq'=64,'tensor'=4] {'tensor'}, use_global_device_ids=true, to_apply=%region_8.9 | all-reduce | flops 10240 | bytes 81920 | tf_op jit(solution)/shard_map/psum | solution.py:104
  162.0 0.1 multiply_reduce_fusion.2
  162.1 0.2 multiply_reduce_fusion.1
  162.3 0.7 fusion.13
  (36 shorter events, 0.8 us)
Async XLA Ops:
  6.5 13.7 %copy-start = (bf16[1280,3,320]{0,2,1:T(8,128)(2,1)S(1)}, bf16[1280,3,320]{0,2,1:T(8,128)(2,1)}, u32[]{:S(2)}) copy-start(bf16[1280,3,320]{0,2,1:T(8,128)(2,1)} %param.10) | copy-start | bytes 7372804
  20.2 15.3 %copy-start.5 = (s32[24]{0:T(128)S(1)}, s32[24]{0:T(128)}, u32[]{:S(2)}) copy-start(s32[24]{0:T(128)} %param.16) | copy-start | bytes 292
  20.3 15.3 %copy-start.6 = (s32[24]{0:T(128)S(1)}, s32[24]{0:T(128)}, u32[]{:S(2)}) copy-start(s32[24]{0:T(128)} %param.15) | copy-start | bytes 292
  21.0 0.6 copy-start.3
  23.4 25.0 %all-to-all-start = ((bf16[64,2,1280]{2,1,0:T(2,128)(2,1)}), bf16[64,2,1280]{2,1,0:T(2,128)(2,1)S(1)}, u32[]{:S(2)}, u32[]{:S(2)}) async-start(bf16[64,2,1280]{2,1,0:T(2,128)(2,1)} %reshape.197), calls=%async_computation | async-start | bytes 655360 | tf_op jit(solution)/shard_map/all_to_all | solution.py:54
  35.5 94.6 %all-gather.3.cloned.1.call-start = ((), (), s32[]{:S(2)}) async-start(), calls=%async_computation.1 | async-start | bytes 2396160 | tf_op jit(solution)/shard_map/all_gather | solution.py:78
  35.7 4.3 %copy-start.1 = (s32[512]{0:T(512)S(1)}, s32[512]{0:T(512)}, u32[]{:S(2)}) copy-start(s32[512]{0:T(512)} %param.14) | copy-start | bytes 6148
  137.3 6.5 %copy-start.2 = (bf16[320,1280]{1,0:T(8,128)(2,1)S(1)}, bf16[320,1280]{1,0:T(8,128)(2,1)}, u32[]{:S(2)}) copy-start(bf16[320,1280]{1,0:T(8,128)(2,1)} %param.11) | copy-start | bytes 2457604
  140.3 21.8 %copy-start.4 = (f32[1280]{0:T(1024)S(1)}, f32[1280]{0:T(1024)}, u32[]{:S(2)}) copy-start(f32[1280]{0:T(1024)} %param.13) | copy-start | bytes 15364
Sparse Core Ops, SparseCore 0:
  56.9 73.1 all-gather.2
